TPU v7x, 256 devices: a whole 4x4x8 slice. The times are simulated.
256 devices in a mesh: expert: 16 (over z, core), fsdp: 16 (over x, y).
Axes of the slice: x: 4, y: 4, z: 8, core: 2. Of those that a mesh axis runs over, the one named last changes fastest.
Arguments:
- tokens: bfloat16 [4096, 6144], P(('expert', 'fsdp')), may hold values from -6 to 6
- expert_ids: int32 [4096, 4], P(('expert', 'fsdp')), may hold values from 0 to 15, all different within a row; in each aligned block of 16 rows (0 to 15, 16 to 31, ...) at most 5 rows name the same one
- router_weight: float32 [4096, 4], P(('expert', 'fsdp')), may hold values from 0.1 to 1
- w_gate: bfloat16 [16, 5376, 6144], P('expert', 'fsdp'), may hold values from -0.078125 to 0.078125
- w_up: bfloat16 [16, 5376, 6144], P('expert', 'fsdp'), may hold values from -0.078125 to 0.078125
Outputs:
- routed: bfloat16 [4096, 4, 5376], P(('expert', 'fsdp'))
Inputs may be any that keep to these rules, and one draw needn't show every extreme that they name: `expert_ids`: each row names 4 different experts; the 16 rows of one device name any one expert at most 5 times, and some device names some expert exactly 5 times.
All inputs are finite; a program needn't handle non-finite values.
Results may differ from a plain program's by a relative error of at most 0.0049.
Values may be sent and summed in bfloat16 or wider, within the bound.
No kernel may reach another device: no remote copies, remote signals or barrier semaphores. Data moves between devices by JAX's collectives and lax.ppermute only.
A program may use at most 128 MiB of HBM per device.

v0:
```python
import jax
import jax.numpy as jnp
from jax import lax
from jax.sharding import PartitionSpec as P


def hidden_block(row_block, gate_rows, up_rows):
    gate_act = lax.dot_general(
        row_block, gate_rows, (((1,), (1,)), ((), ())), preferred_element_type=jnp.float32
    )
    up_act = lax.dot_general(
        row_block, up_rows, (((1,), (1,)), ((), ())), preferred_element_type=jnp.float32
    )
    return (jax.nn.gelu(gate_act, approximate=False) * up_act).astype(jnp.bfloat16)


def local(tokens, expert_ids, router_weight, w_gate, w_up):
    tok_rows, model_width = tokens.shape
    top_count = expert_ids.shape[1]
    experts = lax.axis_size("expert")
    fsdp_size = lax.axis_size("fsdp")
    cap_slots = 5 * tok_rows * top_count // (4 * experts)
    flat_ids = expert_ids.reshape(-1)
    choosing = (flat_ids[:, None] == jnp.arange(experts, dtype=jnp.int32)[None, :]).astype(
        jnp.int32
    )
    slot_rank = jnp.sum((jnp.cumsum(choosing, axis=0) - 1) * choosing, axis=1)
    slot_of = flat_ids * cap_slots + slot_rank
    placing = (
        slot_of[None, :] == jnp.arange(experts * cap_slots, dtype=jnp.int32)[:, None]
    ).astype(jnp.bfloat16)
    repeated = jnp.repeat(tokens, top_count, axis=0)
    outgoing = jnp.dot(placing, repeated, preferred_element_type=jnp.float32).astype(jnp.bfloat16)
    outgoing = outgoing.reshape(experts, cap_slots, model_width)
    gate_rows = w_gate[0]
    up_rows = w_up[0]
    columns = gate_rows.shape[0]
    arrived = lax.all_to_all(outgoing, "expert", split_axis=0, concat_axis=0, tiled=True)
    local_hidden = hidden_block(
        lax.all_gather(arrived.reshape(-1, model_width), "fsdp", axis=0, tiled=True),
        gate_rows,
        up_rows,
    )
    shaped = local_hidden.reshape(fsdp_size, experts, cap_slots, columns)
    step_one = lax.all_to_all(shaped, "expert", split_axis=1, concat_axis=1, tiled=True)
    returned = lax.all_to_all(step_one, "fsdp", split_axis=0, concat_axis=3, tiled=True)
    returned = returned.reshape(experts * cap_slots, -1)
    collected = lax.dot_general(
        placing, returned, (((0,), (0,)), ((), ())), preferred_element_type=jnp.float32
    )
    routed = (router_weight.reshape(-1, 1) * collected).astype(jnp.bfloat16)
    return routed.reshape(tok_rows, top_count, -1)


def solution(mesh):
    return jax.shard_map(
        local,
        mesh=mesh,
        in_specs=(
            P(("expert", "fsdp"), None),
            P(("expert", "fsdp"), None),
            P(("expert", "fsdp"), None),
            P("expert", "fsdp", None),
            P("expert", "fsdp", None),
        ),
        out_specs=P(("expert", "fsdp"), None, None),
        check_vma=False,
    )
```

profile of v0, /device:TPU:1, one launch (start us, length us, event | category | flops | bytes accessed | tf_op | source)
XLA Modules:
  0.0 259.9 jit_solution(14394430911966610535)
XLA Ops:
  6.5 0.0 all-gather.2.cloned.1.call-start
  6.5 0.8 copy.13
  7.3 0.1 reshape.33
  7.4 0.1 fusion.20
  7.5 0.1 reduce_window_sum.11
  7.6 0.2 select_reduce_fusion
  7.8 1.2 broadcast_in_dim.2
  9.0 0.2 reshape.34
  9.2 0.4 convolution_convert_fusion
  9.6 0.5 reshape.35
  10.1 49.6 %all_to_all.25 = bf16[16,5,6144]{2,1,0:T(8,128)(2,1)S(1)} all-to-all(bf16[16,5,6144]{2,1,0:T(8,128)(2,1)S(1)} %reshape.35), channel_id=1, replica_groups=mesh['expert'=16,'fsdp'=16] {'expert'}, dimensions={0} | all-to-all | bytes 1966080 | tf_op jit(solution)/shard_map/all_to_all | solution.py:38
  59.6 1.2 reshape.36
  60.9 0.0 all-gather.2.cloned.1.call-update
  60.9 107.8 %all-gather.2.cloned.1.call-done = bf16[1280,6144]{1,0:T(8,128)(2,1)} async-done(((bf16[80,6144]{1,0:T(8,128)(2,1)}), bf16[1280,6144]{1,0:T(8,128)(2,1)}) %all-gather.2.cloned.1.call-update) | async-done | bytes 15728656 | tf_op jit(solution)/shard_map/all_gather | solution.py:40
  168.7 0.0 copy-start.1
  168.7 0.0 copy-start.2
  168.7 11.7 %fusion.3 = f32[1280,336]{0,1:T(8,128)S(1)} fusion(bf16[1280,6144]{1,0:T(8,128)(2,1)} %all-gather.2.cloned.1.call-done, bf16[1,336,6144]{2,1,0:T(8,128)(2,1)} %param.8), kind=kOutput, calls=%fused_computation.5 | convolution fusion | flops 5284823040 | bytes 21577728 | tf_op jit(solution)/shard_map/dot_general | solution.py:8
  180.5 0.0 copy-done.1
  180.5 0.5 copy-done.2
  181.0 8.9 %fusion.8 = bf16[1280,336]{0,1:T(8,128)(2,1)S(1)} fusion(bf16[1280,6144]{1,0:T(8,128)(2,1)S(1)} %copy-done.1, bf16[1,336,6144]{2,1,0:T(8,128)(2,1)S(1)} %copy-done.2, f32[1280,336]{0,1:T(8,128)S(1)} %fusion.3), kind=kOutput, calls=%fused_computation.8 | convolution fusion | flops 5313208320 | bytes 22437888 | tf_op jit(solution)/shard_map/dot_general | solution.py:11
  190.0 0.6 copy.14
  190.6 0.7 reshape.37
  191.3 0.7 copy.15
  192.0 34.7 %all_to_all.26 = bf16[16,16,5,336]{3,0,2,1:T(8,128)(2,1)S(1)} all-to-all(bf16[16,16,5,336]{3,0,2,1:T(8,128)(2,1)S(1)} %copy.15), channel_id=1, replica_groups=mesh['expert'=16,'fsdp'=16] {'expert'}, dimensions={1} | all-to-all | bytes 1720320 | tf_op jit(solution)/shard_map/all_to_all | solution.py:45
  226.7 0.0 copy-start
  226.7 1.2 copy.16
  227.8 5.0 %all-to-all-start.2 = ((bf16[16,16,5,336]{3,1,2,0:T(8,128)(2,1)}), bf16[16,16,5,336]{3,1,2,0:T(8,128)(2,1)S(1)}, u32[]{:S(2)}, u32[]{:S(2)}) async-start(bf16[16,16,5,336]{3,1,2,0:T(8,128)(2,1)} %copy.16), calls=%async_computation.2 | async-start | bytes 1966080 | tf_op jit(solution)/shard_map/all_to_all | solution.py:46
  232.8 0.0 copy-done
  232.8 0.1 copy.12
  232.9 0.1 mul.41
  233.0 17.3 %all-to-all-done.2 = bf16[16,16,5,336]{3,1,2,0:T(8,128)(2,1)S(1)} async-done(((bf16[16,16,5,336]{3,1,2,0:T(8,128)(2,1)}), bf16[16,16,5,336]{3,1,2,0:T(8,128)(2,1)S(1)}, u32[]{:S(2)}, u32[]{:S(2)}) %all-to-all-start.2) | async-done | bytes 860192 | tf_op jit(solution)/shard_map/all_to_all | solution.py:46
  250.3 0.2 copy.17
  250.5 1.2 reshape.38
  251.7 0.4 fusion
  252.1 1.0 reshape.39
  (1 shorter events, 0.0 us)
Async XLA Ops:
  6.5 162.2 %all-gather.2.cloned.1.call-start = ((), (), s32[]{:S(2)}) async-start(), calls=%async_computation.3 | async-start | bytes 16711680 | tf_op jit(solution)/shard_map/all_gather | solution.py:40
  168.7 11.8 %copy-start.1 = (bf16[1280,6144]{1,0:T(8,128)(2,1)S(1)}, bf16[1280,6144]{1,0:T(8,128)(2,1)}, u32[]{:S(2)}) copy-start(bf16[1280,6144]{1,0:T(8,128)(2,1)} %all-gather.2.cloned.1.call-done) | copy-start | bytes 47185924
  168.7 12.3 %copy-start.2 = (bf16[1,336,6144]{2,1,0:T(8,128)(2,1)S(1)}, bf16[1,336,6144]{2,1,0:T(8,128)(2,1)}, u32[]{:S(2)}) copy-start(bf16[1,336,6144]{2,1,0:T(8,128)(2,1)} %param.9) | copy-start | bytes 12386308
  226.7 6.2 %copy-start = (f32[16,4]{0,1:T(4,128)S(1)}, f32[16,4]{0,1:T(4,128)}, u32[]{:S(2)}) copy-start(f32[16,4]{0,1:T(4,128)} %param.7) | copy-start | bytes 772
  227.8 22.5 %all-to-all-start.2 = ((bf16[16,16,5,336]{3,1,2,0:T(8,128)(2,1)}), bf16[16,16,5,336]{3,1,2,0:T(8,128)(2,1)S(1)}, u32[]{:S(2)}, u32[]{:S(2)}) async-start(bf16[16,16,5,336]{3,1,2,0:T(8,128)(2,1)} %copy.16), calls=%async_computation.2 | async-start | bytes 1966080 | tf_op jit(solution)/shard_map/all_to_all | solution.py:46
Sparse Core Ops, SparseCore 0:
  61.0 107.6 all-gather.1
where the time goes:
time: 260 us
  waiting for transfers between devices  125 us (48%)
  blocking collectives  84.3 us (32%)
  matrix products  21.5 us (8%)
  between operations  13.5 us (5%)
  local copies, waits for them, and re-layouts  10.2 us (4%)
  starting transfers between devices  4.97 us (2%)
    all_gather x1, waiting for transfers between devices, local(): lax.all_gather(arrived.reshape(-1, model_width), 'fsdp', axis=0, tiled=True)  108 us
    all_to_all x1, blocking collectives, local(): lax.all_to_all(outgoing, 'expert', split_axis=0, concat_axis=0, tiled=True)  49.6 us
    all_to_all x1, blocking collectives, local(): lax.all_to_all(shaped, 'expert', split_axis=1, concat_axis=1, tiled=True)  34.7 us
    all_to_all x1, waiting for transfers between devices, local(): lax.all_to_all(step_one, 'fsdp', split_axis=0, concat_axis=3, tiled=True)  17.3 us
    dot_general x1, matrix products, hidden_block(): lax.dot_general(row_block, gate_rows, (((1,), (1,)), ((), ())), preferred...  11.7 us
    dot_general x1, matrix products, hidden_block(): lax.dot_general(row_block, up_rows, (((1,), (1,)), ((), ())), preferred_e...  8.93 us
  transfers between devices with their start and end apart: 2, of which 2 were waited for; matrix products, arithmetic and copies ran while one was open for 0% of the time, Pallas kernels for 0%

commit v1 on v0

--- a/solution.py
+++ b/solution.py
@@ -37,7 +37,12 @@
     columns = gate_rows.shape[0]
     arrived = lax.all_to_all(outgoing, "expert", split_axis=0, concat_axis=0, tiled=True)
     local_hidden = hidden_block(
-        lax.all_gather(arrived.reshape(-1, model_width), "fsdp", axis=0, tiled=True),
+        jnp.concatenate(
+            lax.all_to_all(
+                jnp.stack([arrived.reshape(-1, model_width)] * lax.axis_size("fsdp")), "fsdp", 0, 0
+            ),
+            axis=0,
+        ),
         gate_rows,
         up_rows,
     )

time: 260 us -> 316 us (1.22)
  blocking collectives: 84.3 us -> 261 us
  waiting for transfers between devices: 125 us -> 17.3 us
  between operations: 13.5 us -> 0.15 us
    all_to_all x0 -> x1, blocking collectives: none -> 181 us  [local(): lax.all_to_all(jnp.stack([arrived.reshape(-1, model_width)] * lax.axis_si...]
    all_gather x1 -> x0, waiting for transfers between devices: 108 us -> none  [local(): lax.all_gather(arrived.reshape(-1, model_width), 'fsdp', axis=0, tiled=True)]
    dot_general x1, matrix products: 8.93 us -> 15.7 us  [hidden_block(): lax.dot_general(row_block, up_rows, (((1,), (1,)), ((), ())), preferred_e...]
    dot_general x1, matrix products: 11.7 us -> 5.58 us  [hidden_block(): lax.dot_general(row_block, gate_rows, (((1,), (1,)), ((), ())), preferred...]
    all_to_all x1, blocking collectives: 34.7 us -> 30.6 us  [local(): lax.all_to_all(shaped, 'expert', split_axis=1, concat_axis=1, tiled=True)]
  transfers between devices with their start and end apart: 2 -> 1, of which waited for: 2 -> 1; matrix products, arithmetic and copies ran while one was open for 0% -> 0% of each run, Pallas kernels for 0% -> 0%
where the time goes in v1:
time: 316 us
  blocking collectives  261 us (83%)
  matrix products  22.1 us (7%)
  waiting for transfers between devices  17.3 us (5%)
  local copies, waits for them, and re-layouts  10.7 us (3%)
  starting transfers between devices  3.72 us (1%)
    all_to_all x1, blocking collectives, local(): lax.all_to_all(jnp.stack([arrived.reshape(-1, model_width)] * lax.axis_si...  181 us
    all_to_all x1, blocking collectives, local(): lax.all_to_all(outgoing, 'expert', split_axis=0, concat_axis=0, tiled=True)  49.6 us
    all_to_all x1, blocking collectives, local(): lax.all_to_all(shaped, 'expert', split_axis=1, concat_axis=1, tiled=True)  30.6 us
    all_to_all x1, waiting for transfers between devices, local(): lax.all_to_all(step_one, 'fsdp', split_axis=0, concat_axis=3, tiled=True)  17.3 us
    dot_general x1, matrix products, hidden_block(): lax.dot_general(row_block, up_rows, (((1,), (1,)), ((), ())), preferred_e...  15.7 us
  transfers between devices with their start and end apart: 1, of which 1 were waited for; matrix products, arithmetic and copies ran while one was open for 0% of the time, Pallas kernels for 0%

profile of v1, /device:TPU:1, one launch (start us, length us, event | category | flops | bytes accessed | tf_op | source)
XLA Modules:
  0.0 315.5 jit_solution(16552657904555648732)
XLA Ops:
  0.0 0.8 copy.13
  0.8 0.1 reshape.35
  0.8 0.1 fusion.20
  0.9 0.1 reduce_window_sum.11
  1.0 0.2 select_reduce_fusion
  1.2 1.2 broadcast_in_dim.2
  2.5 0.2 reshape.36
  2.6 0.4 convolution_convert_fusion
  3.0 0.5 reshape.37
  3.5 49.6 %all_to_all.30 = bf16[16,5,6144]{2,1,0:T(8,128)(2,1)S(1)} all-to-all(bf16[16,5,6144]{2,1,0:T(8,128)(2,1)S(1)} %reshape.37), channel_id=1, replica_groups=mesh['expert'=16,'fsdp'=16] {'expert'}, dimensions={0} | all-to-all | bytes 1966080 | tf_op jit(solution)/shard_map/all_to_all | solution.py:38
  53.1 0.5 stack_reshape.2
  53.6 2.0 stack.3
  55.6 0.0 copy-start.1
  55.6 181.0 %all_to_all.31 = bf16[16,80,6144]{2,1,0:T(8,128)(2,1)S(1)} all-to-all(bf16[16,80,6144]{2,1,0:T(8,128)(2,1)S(1)} %stack.3), channel_id=1, replica_groups=mesh['expert'=16,'fsdp'=16] {'fsdp'}, dimensions={0} | all-to-all | bytes 31457280 | tf_op jit(solution)/shard_map/all_to_all | solution.py:41
  236.6 0.0 copy-done.1
  236.6 5.6 %fusion.3 = f32[1280,336]{0,1:T(8,128)S(1)} fusion(bf16[1280,6144]{1,0:T(8,128)(2,1)S(1)} %bitcast.20, bf16[1,336,6144]{2,1,0:T(8,128)(2,1)S(1)} %copy-done.1), kind=kOutput, calls=%fused_computation.5 | convolution fusion | flops 5284823040 | bytes 21577728 | tf_op jit(solution)/shard_map/dot_general | solution.py:8
  242.2 15.7 %fusion.8 = bf16[1280,336]{0,1:T(8,128)(2,1)S(1)} fusion(bf16[1280,6144]{1,0:T(8,128)(2,1)S(1)} %bitcast.21, bf16[1,336,6144]{2,1,0:T(8,128)(2,1)} %param.9, f32[1280,336]{0,1:T(8,128)S(1)} %fusion.3), kind=kOutput, calls=%fused_computation.8 | convolution fusion | flops 5313208320 | bytes 22437888 | tf_op jit(solution)/shard_map/dot_general | solution.py:11
  258.0 0.6 copy.14
  258.6 0.5 reshape.39
  259.1 0.7 copy.15
  259.8 30.6 %all_to_all.32 = bf16[16,16,5,336]{3,0,2,1:T(8,128)(2,1)S(1)} all-to-all(bf16[16,16,5,336]{3,0,2,1:T(8,128)(2,1)S(1)} %copy.15), channel_id=1, replica_groups=mesh['expert'=16,'fsdp'=16] {'expert'}, dimensions={1} | all-to-all | bytes 1720320 | tf_op jit(solution)/shard_map/all_to_all | solution.py:50
  290.4 0.0 copy-start
  290.4 1.2 copy.16
  291.5 3.7 %all-to-all-start.3 = ((bf16[16,16,5,336]{3,1,2,0:T(8,128)(2,1)}), bf16[16,16,5,336]{3,1,2,0:T(8,128)(2,1)S(1)}, u32[]{:S(2)}, u32[]{:S(2)}) async-start(bf16[16,16,5,336]{3,1,2,0:T(8,128)(2,1)} %copy.16), calls=%async_computation.3 | async-start | bytes 1966080 | tf_op jit(solution)/shard_map/all_to_all | solution.py:51
  295.2 0.0 copy-done
  295.3 0.1 copy.12
  295.3 0.1 mul.41
  295.4 17.3 %all-to-all-done.3 = bf16[16,16,5,336]{3,1,2,0:T(8,128)(2,1)S(1)} async-done(((bf16[16,16,5,336]{3,1,2,0:T(8,128)(2,1)}), bf16[16,16,5,336]{3,1,2,0:T(8,128)(2,1)S(1)}, u32[]{:S(2)}, u32[]{:S(2)}) %all-to-all-start.3) | async-done | bytes 860192 | tf_op jit(solution)/shard_map/all_to_all | solution.py:51
  312.7 0.2 copy.17
  312.9 1.2 reshape.40
  314.1 0.4 fusion
  314.5 1.0 reshape.41
  (1 shorter events, 0.0 us)
Async XLA Ops:
  55.6 181.0 %copy-start.1 = (bf16[1,336,6144]{2,1,0:T(8,128)(2,1)S(1)}, bf16[1,336,6144]{2,1,0:T(8,128)(2,1)}, u32[]{:S(2)}) copy-start(bf16[1,336,6144]{2,1,0:T(8,128)(2,1)} %param.8) | copy-start | bytes 12386308
  290.4 4.9 %copy-start = (f32[16,4]{0,1:T(4,128)S(1)}, f32[16,4]{0,1:T(4,128)}, u32[]{:S(2)}) copy-start(f32[16,4]{0,1:T(4,128)} %param.7) | copy-start | bytes 772
  291.5 21.2 %all-to-all-start.3 = ((bf16[16,16,5,336]{3,1,2,0:T(8,128)(2,1)}), bf16[16,16,5,336]{3,1,2,0:T(8,128)(2,1)S(1)}, u32[]{:S(2)}, u32[]{:S(2)}) async-start(bf16[16,16,5,336]{3,1,2,0:T(8,128)(2,1)} %copy.16), calls=%async_computation.3 | async-start | bytes 1966080 | tf_op jit(solution)/shard_map/all_to_all | solution.py:51
